TPU v7x, 32 devices: a whole 2x2x4 slice. The times are simulated.
32 devices in a mesh: gx: 4 (over z), gy: 2 (over y), gz: 4 (over x, core).
Axes of the slice: x: 2, y: 2, z: 4, core: 2. Of those that a mesh axis runs over, the one named last changes fastest.
Arguments:
- positions: float32 [3, 4, 2, 8, 128], P(None, 'gx', 'gy', 'gz'), may hold values from 0 to 8, as said below
- velocity: float32 [3, 4, 2, 8, 128], P(None, 'gx', 'gy', 'gz'), may hold values from -16 to 16
- counts: int32 [4, 2, 8], P('gx', 'gy', 'gz'), may hold values from 0 to 128, as said below
Outputs:
- velocity_new: float32 [3, 4, 2, 8, 128], P(None, 'gx', 'gy', 'gz')
- pressure: float32 [4, 2, 8, 128], P('gx', 'gy', 'gz')
Inputs may be any that keep to these rules, and one draw needn't show every extreme that they name: `positions`: component k of the position of any slot of tile (a, b, c) lies in [t, t + 1), where t is a, b or c for k = 0, 1, 2. A tile's particles fill its first counts[a, b, c] slots. In every column of tiles the bottom tile is full, the tiles below one topmost wet tile hold 96 or more particles, and the tiles above it are empty.
All inputs are finite; a program needn't handle non-finite values.
Results may differ from a plain program's by a relative error of at most 0.0003.
Values sent between devices are 32-bit elements; how exact they have to be, the bound alone decides.
No kernel may reach another device: no remote copies, remote signals or barrier semaphores. Data moves between devices by JAX's collectives and lax.ppermute only.
A program may use at most 64 MiB of HBM per device.

v0:
```python
import jax
import jax.numpy as jnp
from jax import lax
from jax.sharding import PartitionSpec as P

ITERS = 3
DIAG_SHIFT = 0.05
VISCOSITY = 0.5
GRAVITY = 0.1
GRADIENT_GAIN = 32.0
AXES = (("gx", 1), ("gy", 2), ("gz", 3))


def with_halo(cells, sides, width):
    for axis, dim in sides:
        count = lax.axis_size(axis)
        ends = count - 1
        head = lax.slice_in_dim(cells, 0, width, axis=dim)
        tail = lax.slice_in_dim(cells, cells.shape[dim] - width, cells.shape[dim], axis=dim)
        cells = jnp.concatenate(
            [
                lax.ppermute(tail, axis, [(i, (i + 1) % count) for i in range(ends)]),
                cells,
                lax.ppermute(head, axis, [((i + 1) % count, i) for i in range(ends)]),
            ],
            axis=dim,
        )
    return cells


def neighbours(rim):
    comps, size_x, size_y, size_z, width = rim.shape
    blocks = []
    for ax in range(size_x - 2):
        for ay in range(size_y - 2):
            for az in range(size_z - 2):
                window = rim[:, ax : ax + 3, ay : ay + 3, az : az + 3, :]
                blocks.append(window.reshape(comps, 27 * width))
    return jnp.stack(blocks, axis=1)


def flat(cells):
    return cells.reshape(cells.shape[0], -1, cells.shape[4])


def wsum(weight, near):
    return jnp.sum(weight[None] * near[:, :, None, :], axis=-1)


def tile_corners(block_shape):
    _, size_x, size_y, size_z, _ = block_shape
    base = (
        lax.axis_index("gx") * size_x,
        lax.axis_index("gy") * size_y,
        lax.axis_index("gz") * size_z,
    )
    corners = []
    for ax in range(size_x):
        for ay in range(size_y):
            for az in range(size_z):
                corners.append(jnp.stack([base[0] + ax, base[1] + ay, base[2] + az]))
    return jnp.stack(corners, axis=1).astype(jnp.float32)


def on_device(positions, velocity, counts):
    block_shape = positions.shape
    width = positions.shape[4]
    slot_ids = jnp.arange(width, dtype=jnp.int32)
    valid_mask = (slot_ids[None, None, None, :] < counts[:, :, :, None]).astype(jnp.float32)[None]
    packed = jnp.concatenate([positions, valid_mask, velocity], axis=0)
    near_all = neighbours(with_halo(packed, AXES, 1))
    near_x = near_all[0:3]
    near_valid = near_all[3]
    near_v = near_all[4:7]
    own_x = flat(positions)
    own_valid = flat(valid_mask)[0]
    own_v = flat(velocity)
    offset = own_x[:, :, :, None] - near_x[:, :, None, :]
    distance = offset[0] * offset[0] + offset[1] * offset[1] + offset[2] * offset[2]
    closeness = jnp.maximum(1.0 - distance, 0.0)
    weight = closeness * closeness * own_valid[:, :, None] * near_valid[:, None, :]
    corner = tile_corners(block_shape)[:, :, None]
    local_own = own_x - corner
    local_near = near_x - corner
    row = jnp.sum(weight, axis=-1)[None]
    sums = wsum(weight, jnp.concatenate([near_v, local_near], axis=0))
    near_sums = sums[0:3]
    lever = local_own * row - sums[3:6]
    gravity_pull = jnp.array([0.0, 0.0, -GRAVITY], jnp.float32).reshape(3, 1, 1)
    predicted = own_valid[None] * (
        own_v + VISCOSITY / width * (near_sums - row * own_v) + gravity_pull
    )
    diagonal = DIAG_SHIFT + row / width

    def shaped(values):
        return values.reshape(values.shape[0], *block_shape[1:])

    near_pred = neighbours(with_halo(shaped(predicted), AXES, 1))
    dotted = jnp.sum(near_pred * local_near, axis=0, keepdims=True)
    psums = wsum(weight, jnp.concatenate([near_pred, dotted], axis=0))
    flux = jnp.sum(local_own * psums[0:3], axis=0, keepdims=True) - psums[3:4]
    source = -(GRADIENT_GAIN / width) * (jnp.sum(predicted * lever, axis=0, keepdims=True) - flux)

    def operate(field):
        near_field = neighbours(with_halo(shaped(field), AXES, 1))
        return (near_field, diagonal * field - wsum(weight, near_field) / width)

    def paired_sums(residual, precond, applied):
        pair = jnp.stack([jnp.sum(residual * precond), jnp.sum(precond * applied)])
        total = lax.psum(pair, ("gx", "gy", "gz"))
        return (total[0], total[1])

    pressure = jnp.zeros_like(source)
    residual = source
    precond = residual / diagonal
    near_dir, applied = operate(precond)
    norm_now, curvature_sum = paired_sums(residual, precond, applied)
    step_size = norm_now / curvature_sum
    direction = precond
    along = applied
    near_pressure = jnp.zeros_like(near_dir)
    for iteration in range(ITERS):
        pressure = pressure + step_size * direction
        near_pressure = near_pressure + step_size * near_dir
        residual = residual - step_size * along
        if iteration + 1 < ITERS:
            precond = residual / diagonal
            near_fresh, applied = operate(precond)
            norm_next, curvature_sum = paired_sums(residual, precond, applied)
            blend = norm_next / norm_now
            step_size = norm_next / (curvature_sum - blend * norm_next / step_size)
            direction = precond + blend * direction
            near_dir = near_fresh + blend * near_dir
            along = applied + blend * along
            norm_now = norm_next
    grads = wsum(weight, jnp.concatenate([near_pressure, near_pressure * local_near], axis=0))
    moments = local_own * grads[0:1] - grads[1:4]
    velocity_new = predicted - GRADIENT_GAIN / width * (pressure * lever - moments)
    return (shaped(velocity_new), shaped(pressure)[0])


def solution(mesh):
    in_specs = (
        P(None, "gx", "gy", "gz", None),
        P(None, "gx", "gy", "gz", None),
        P("gx", "gy", "gz"),
    )
    out_specs = (P(None, "gx", "gy", "gz", None), P("gx", "gy", "gz", None))
    return jax.shard_map(
        on_device, mesh=mesh, in_specs=in_specs, out_specs=out_specs, check_vma=False
    )
```

profile of v0, /device:TPU:0, one launch (start us, length us, event | category | flops | bytes accessed | tf_op | source)
XLA Modules:
  0.0 319.3 jit_solution(7614055411883678423)
XLA Ops:
  4.0 5.6 %collective-permute-start = (f32[7,1,1,2,128]{4,0,3,2,1:T(8,128)S(1)}, f32[7,1,1,2,128]{4,0,3,2,1:T(8,128)S(1)}, u32[]{:S(2)}, u32[]{:S(2)}) collective-permute-start(f32[7,1,1,2,128]{4,0,3,2,1:T(8,128)S(1)} %pad_maximum_fusion.19), channel_id=1, source_target_pairs={{0,8},{8,16},{16,24},{1,9},{9,17},{17,25},{2,10},{10,18},{18,26},{... | collective-permute-start | bytes 21512 | tf_op jit(solution)/shard_map/ppermute | solution.py:22
  12.3 4.5 %collective-permute-start.2 = (f32[7,3,1,2,128]{4,0,3,2,1:T(8,128)S(1)}, f32[7,3,1,2,128]{4,0,3,2,1:T(8,128)S(1)}, u32[]{:S(2)}, u32[]{:S(2)}) collective-permute-start(f32[7,3,1,2,128]{4,0,3,2,1:T(8,128)S(1)} %pad_maximum_fusion.11), channel_id=1, source_target_pairs={{0,4},{1,5},{2,6},{3,7},{8,12},{9,13},{10,14},{11,15},{16,20},{17,... | collective-permute-start | bytes 64520 | tf_op jit(solution)/shard_map/ppermute | solution.py:22
  21.0 3.9 %collective-permute-done.5 = f32[7,3,3,1,128]{4,0,3,2,1:T(8,128)S(1)} collective-permute-done((f32[7,3,3,1,128]{4,0,3,2,1:T(8,128)S(1)}, f32[7,3,3,1,128]{4,0,3,2,1:T(8,128)S(1)}, u32[]{:S(2)}, u32[]{:S(2)}) %collective-permute-start.5) | collective-permute-done | bytes 32288 | tf_op jit(solution)/shard_map/ppermute | solution.py:24
  25.7 1.5 broadcast_subtract_fusion
  27.2 1.6 fusion.6
  29.3 1.7 copy-done
  31.0 1.8 multiply_reduce_fusion
  34.2 4.8 %collective-permute-start.6 = (f32[3,1,1,2,128]{4,3,0,2,1:T(2,128)S(1)}, f32[3,1,1,2,128]{4,3,0,2,1:T(2,128)S(1)}, u32[]{:S(2)}, u32[]{:S(2)}) collective-permute-start(f32[3,1,1,2,128]{4,3,0,2,1:T(2,128)S(1)} %bitcast.144), channel_id=1, source_target_pairs={{0,8},{8,16},{16,24},{1,9},{9,17},{17,25},{2,10},{10,18},{18,26},{... | collective-permute-start | bytes 9224 | tf_op jit(solution)/shard_map/ppermute | solution.py:22
  41.7 4.5 %collective-permute-start.8 = (f32[3,3,1,2,128]{4,3,0,2,1:T(2,128)S(1)}, f32[3,3,1,2,128]{4,3,0,2,1:T(2,128)S(1)}, u32[]{:S(2)}, u32[]{:S(2)}) collective-permute-start(f32[3,3,1,2,128]{4,3,0,2,1:T(2,128)S(1)} %pad_maximum_fusion.15), channel_id=1, source_target_pairs={{0,4},{1,5},{2,6},{3,7},{8,12},{9,13},{10,14},{11,15},{16,20},{17,... | collective-permute-start | bytes 27656 | tf_op jit(solution)/shard_map/ppermute | solution.py:22
  49.5 3.8 %collective-permute-start.10 = (f32[3,3,3,1,128]{4,3,0,2,1:T(1,128)}, f32[3,3,3,1,128]{4,3,0,2,1:T(1,128)}, u32[]{:S(2)}, u32[]{:S(2)}) collective-permute-start(f32[3,3,3,1,128]{4,3,0,2,1:T(1,128)} %get-tuple-element.28), channel_id=1, source_target_pairs={{0,1},{1,2},{2,3},{4,5},{5,6},{6,7},{8,9},{9,10},{10,11},{12,13},{... | collective-permute-start | bytes 41480 | tf_op jit(solution)/shard_map/ppermute | solution.py:22
  54.7 1.5 pad_maximum_fusion.5
  56.8 1.5 stack_reshape.32
  61.1 1.5 stack_reshape.33
  62.6 1.4 constant_dynamic-update-slice_fusion
  66.1 3.3 %multiply_reduce_fusion.2 = f32[4,2,128]{2,1,0:T(2,128)S(1)} fusion(f32[4,2,3456]{2,1,0:T(2,128)S(1)} %copy.34, f32[2,128,3456]{2,1,0:T(8,128)} %copy-done), kind=kLoop, calls=%fused_computation.2 | loop fusion | flops 7076864 | bytes 3653632 | tf_op jit(solution)/shard_map/reduce_sum | solution.py:47
  71.4 4.6 %collective-permute-start.12 = (f32[1,1,1,2,128]{4,3,2,1,0:T(2,128)S(1)}, f32[1,1,1,2,128]{4,3,2,1,0:T(2,128)S(1)}, u32[]{:S(2)}, u32[]{:S(2)}) collective-permute-start(f32[1,1,1,2,128]{4,3,2,1,0:T(2,128)S(1)} %bitcast.160), channel_id=1, source_target_pairs={{0,8},{8,16},{16,24},{1,9},{9,17},{17,25},{2,10},{10,18},{18,26},{... | collective-permute-start | bytes 3080 | tf_op jit(solution)/shard_map/ppermute | solution.py:22
  78.6 4.5 %collective-permute-start.14 = (f32[1,3,1,2,128]{4,3,2,1,0:T(2,128)S(1)}, f32[1,3,1,2,128]{4,3,2,1,0:T(2,128)S(1)}, u32[]{:S(2)}, u32[]{:S(2)}) collective-permute-start(f32[1,3,1,2,128]{4,3,2,1,0:T(2,128)S(1)} %pad_maximum_fusion.20), channel_id=1, source_target_pairs={{0,4},{1,5},{2,6},{3,7},{8,12},{9,13},{10,14},{11,15},{16,20},{17,... | collective-permute-start | bytes 9224 | tf_op jit(solution)/shard_map/ppermute | solution.py:22
  84.5 1.5 collective-permute-start.16
  87.3 5.3 %collective-permute-done.17 = f32[1,3,3,1,128]{4,3,2,1,0:T(1,128)S(1)} collective-permute-done((f32[1,3,3,1,128]{4,3,2,1,0:T(1,128)S(1)}, f32[1,3,3,1,128]{4,3,2,1,0:T(1,128)S(1)}, u32[]{:S(2)}, u32[]{:S(2)}) %collective-permute-start.17) | collective-permute-done | bytes 4640 | tf_op jit(solution)/shard_map/ppermute | solution.py:24
  98.8 1.8 pad_maximum_fusion.23
  100.6 43.4 %psum.21 = f32[2]{0:T(128)} all-reduce(f32[2]{0:T(128)} %pad_maximum_fusion.23), channel_id=1, replica_groups=mesh['gx'=4,'gy'=2,'gz'=4] {'gx','gy','gz'}, use_global_device_ids=true, to_apply=%region_9.0 | all-reduce | flops 2 | bytes 16 | tf_op jit(solution)/shard_map/psum | solution.py:110
  148.7 4.5 %collective-permute-start.18 = (f32[1,1,1,2,128]{4,3,2,1,0:T(2,128)S(1)}, f32[1,1,1,2,128]{4,3,2,1,0:T(2,128)S(1)}, u32[]{:S(2)}, u32[]{:S(2)}) collective-permute-start(f32[1,1,1,2,128]{4,3,2,1,0:T(2,128)S(1)} %bitcast.149), channel_id=1, source_target_pairs={{0,8},{8,16},{16,24},{1,9},{9,17},{17,25},{2,10},{10,18},{18,26},{... | collective-permute-start | bytes 3080 | tf_op jit(solution)/shard_map/ppermute | solution.py:22
  155.9 4.5 %collective-permute-start.20 = (f32[1,3,1,2,128]{4,3,2,1,0:T(2,128)S(1)}, f32[1,3,1,2,128]{4,3,2,1,0:T(2,128)S(1)}, u32[]{:S(2)}, u32[]{:S(2)}) collective-permute-start(f32[1,3,1,2,128]{4,3,2,1,0:T(2,128)S(1)} %pad_maximum_fusion.21), channel_id=1, source_target_pairs={{0,4},{1,5},{2,6},{3,7},{8,12},{9,13},{10,14},{11,15},{16,20},{17,... | collective-permute-start | bytes 9224 | tf_op jit(solution)/shard_map/ppermute | solution.py:22
  164.4 4.3 %collective-permute-done.23 = f32[1,3,3,1,128]{4,3,2,1,0:T(1,128)S(1)} collective-permute-done((f32[1,3,3,1,128]{4,3,2,1,0:T(1,128)S(1)}, f32[1,3,3,1,128]{4,3,2,1,0:T(1,128)S(1)}, u32[]{:S(2)}, u32[]{:S(2)}) %collective-permute-start.23) | collective-permute-done | bytes 4640 | tf_op jit(solution)/shard_map/ppermute | solution.py:24
  175.5 1.8 pad_maximum_fusion.24
  177.4 43.4 %psum.22 = f32[2]{0:T(128)} all-reduce(f32[2]{0:T(128)} %pad_maximum_fusion.24), channel_id=1, replica_groups=mesh['gx'=4,'gy'=2,'gz'=4] {'gx','gy','gz'}, use_global_device_ids=true, to_apply=%region_13.0 | all-reduce | flops 2 | bytes 16 | tf_op jit(solution)/shard_map/psum | solution.py:110
  229.1 4.5 %collective-permute-start.24 = (f32[1,1,1,2,128]{4,3,2,1,0:T(2,128)S(1)}, f32[1,1,1,2,128]{4,3,2,1,0:T(2,128)S(1)}, u32[]{:S(2)}, u32[]{:S(2)}) collective-permute-start(f32[1,1,1,2,128]{4,3,2,1,0:T(2,128)S(1)} %bitcast.155), channel_id=1, source_target_pairs={{0,8},{8,16},{16,24},{1,9},{9,17},{17,25},{2,10},{10,18},{18,26},{... | collective-permute-start | bytes 3080 | tf_op jit(solution)/shard_map/ppermute | solution.py:22
  236.3 4.5 %collective-permute-start.26 = (f32[1,3,1,2,128]{4,3,2,1,0:T(2,128)S(1)}, f32[1,3,1,2,128]{4,3,2,1,0:T(2,128)S(1)}, u32[]{:S(2)}, u32[]{:S(2)}) collective-permute-start(f32[1,3,1,2,128]{4,3,2,1,0:T(2,128)S(1)} %pad_maximum_fusion.22), channel_id=1, source_target_pairs={{0,4},{1,5},{2,6},{3,7},{8,12},{9,13},{10,14},{11,15},{16,20},{17,... | collective-permute-start | bytes 9224 | tf_op jit(solution)/shard_map/ppermute | solution.py:22
  242.7 1.9 collective-permute-start.28
  244.6 1.5 collective-permute-start.29
  262.5 45.0 %psum.23 = f32[2]{0:T(128)S(1)} all-reduce(f32[2]{0:T(128)S(1)} %pad_maximum_fusion.25), channel_id=1, replica_groups=mesh['gx'=4,'gy'=2,'gz'=4] {'gx','gy','gz'}, use_global_device_ids=true, to_apply=%region_17.0 | all-reduce | flops 2 | bytes 16 | tf_op jit(solution)/shard_map/psum | solution.py:110
  315.3 3.3 %multiply_reduce_fusion.1 = f32[4,2,128]{2,1,0:T(2,128)S(1)} fusion(f32[4,2,3456]{2,1,0:T(2,128)S(1)} %copy.41, f32[2,128,3456]{2,1,0:T(8,128)} %copy-done), kind=kLoop, calls=%fused_computation.1 | loop fusion | flops 7076864 | bytes 3653632 | tf_op jit(solution)/shard_map/reduce_sum | solution.py:47
  (198 shorter events, 84.8 us)
Async XLA Ops:
  2.7 7.6 %collective-permute-start.1 = (f32[7,1,1,2,128]{4,0,3,2,1:T(8,128)S(1)}, f32[7,1,1,2,128]{4,0,3,2,1:T(8,128)S(1)}, u32[]{:S(2)}, u32[]{:S(2)}) collective-permute-start(f32[7,1,1,2,128]{4,0,3,2,1:T(8,128)S(1)} %pad_maximum_fusion.19), channel_id=1, source_target_pairs={{8,0},{16,8},{24,16},{9,1},{17,9},{25,17},{10,2},{18,10},{26,18},{... | collective-permute-start | bytes 21512 | tf_op jit(solution)/shard_map/ppermute | solution.py:24
  4.0 6.9 %collective-permute-start = (f32[7,1,1,2,128]{4,0,3,2,1:T(8,128)S(1)}, f32[7,1,1,2,128]{4,0,3,2,1:T(8,128)S(1)}, u32[]{:S(2)}, u32[]{:S(2)}) collective-permute-start(f32[7,1,1,2,128]{4,0,3,2,1:T(8,128)S(1)} %pad_maximum_fusion.19), channel_id=1, source_target_pairs={{0,8},{8,16},{16,24},{1,9},{9,17},{17,25},{2,10},{10,18},{18,26},{... | collective-permute-start | bytes 21512 | tf_op jit(solution)/shard_map/ppermute | solution.py:22
  11.0 5.9 %collective-permute-start.3 = (f32[7,3,1,2,128]{4,0,3,2,1:T(8,128)S(1)}, f32[7,3,1,2,128]{4,0,3,2,1:T(8,128)S(1)}, u32[]{:S(2)}, u32[]{:S(2)}) collective-permute-start(f32[7,3,1,2,128]{4,0,3,2,1:T(8,128)S(1)} %pad_maximum_fusion.11), channel_id=1, source_target_pairs={{4,0},{5,1},{6,2},{7,3},{12,8},{13,9},{14,10},{15,11},{20,16},{21,... | collective-permute-start | bytes 64520 | tf_op jit(solution)/shard_map/ppermute | solution.py:24
  12.3 6.1 %collective-permute-start.2 = (f32[7,3,1,2,128]{4,0,3,2,1:T(8,128)S(1)}, f32[7,3,1,2,128]{4,0,3,2,1:T(8,128)S(1)}, u32[]{:S(2)}, u32[]{:S(2)}) collective-permute-start(f32[7,3,1,2,128]{4,0,3,2,1:T(8,128)S(1)} %pad_maximum_fusion.11), channel_id=1, source_target_pairs={{0,4},{1,5},{2,6},{3,7},{8,12},{9,13},{10,14},{11,15},{16,20},{17,... | collective-permute-start | bytes 64520 | tf_op jit(solution)/shard_map/ppermute | solution.py:22
  18.3 2.6 collective-permute-start.4
  19.6 5.3 %collective-permute-start.5 = (f32[7,3,3,1,128]{4,0,3,2,1:T(8,128)S(1)}, f32[7,3,3,1,128]{4,0,3,2,1:T(8,128)S(1)}, u32[]{:S(2)}, u32[]{:S(2)}) collective-permute-start(f32[7,3,3,1,128]{4,0,3,2,1:T(8,128)S(1)} %get-tuple-element.24), channel_id=1, source_target_pairs={{1,0},{2,1},{3,2},{5,4},{6,5},{7,6},{9,8},{10,9},{11,10},{13,12},{... | collective-permute-start | bytes 96776 | tf_op jit(solution)/shard_map/ppermute | solution.py:24
  32.9 60.3 %copy-start.3 = (f32[3,2,128]{2,1,0:T(2,128)}, f32[3,2,128]{2,1,0:T(2,128)S(1)}, u32[]{:S(2)}) copy-start(f32[3,2,128]{2,1,0:T(2,128)S(1)} %fusion.20) | copy-start | bytes 9220
  32.9 6.1 %collective-permute-start.7 = (f32[3,1,1,2,128]{4,3,0,2,1:T(2,128)S(1)}, f32[3,1,1,2,128]{4,3,0,2,1:T(2,128)S(1)}, u32[]{:S(2)}, u32[]{:S(2)}) collective-permute-start(f32[3,1,1,2,128]{4,3,0,2,1:T(2,128)S(1)} %bitcast.143), channel_id=1, source_target_pairs={{8,0},{16,8},{24,16},{9,1},{17,9},{25,17},{10,2},{18,10},{26,18},{... | collective-permute-start | bytes 9224 | tf_op jit(solution)/shard_map/ppermute | solution.py:24
  34.2 6.1 %collective-permute-start.6 = (f32[3,1,1,2,128]{4,3,0,2,1:T(2,128)S(1)}, f32[3,1,1,2,128]{4,3,0,2,1:T(2,128)S(1)}, u32[]{:S(2)}, u32[]{:S(2)}) collective-permute-start(f32[3,1,1,2,128]{4,3,0,2,1:T(2,128)S(1)} %bitcast.144), channel_id=1, source_target_pairs={{0,8},{8,16},{16,24},{1,9},{9,17},{17,25},{2,10},{10,18},{18,26},{... | collective-permute-start | bytes 9224 | tf_op jit(solution)/shard_map/ppermute | solution.py:22
  40.4 5.9 %collective-permute-start.9 = (f32[3,3,1,2,128]{4,3,0,2,1:T(2,128)S(1)}, f32[3,3,1,2,128]{4,3,0,2,1:T(2,128)S(1)}, u32[]{:S(2)}, u32[]{:S(2)}) collective-permute-start(f32[3,3,1,2,128]{4,3,0,2,1:T(2,128)S(1)} %pad_maximum_fusion.15), channel_id=1, source_target_pairs={{4,0},{5,1},{6,2},{7,3},{12,8},{13,9},{14,10},{15,11},{20,16},{21,... | collective-permute-start | bytes 27656 | tf_op jit(solution)/shard_map/ppermute | solution.py:24
  41.7 5.9 %collective-permute-start.8 = (f32[3,3,1,2,128]{4,3,0,2,1:T(2,128)S(1)}, f32[3,3,1,2,128]{4,3,0,2,1:T(2,128)S(1)}, u32[]{:S(2)}, u32[]{:S(2)}) collective-permute-start(f32[3,3,1,2,128]{4,3,0,2,1:T(2,128)S(1)} %pad_maximum_fusion.15), channel_id=1, source_target_pairs={{0,4},{1,5},{2,6},{3,7},{8,12},{9,13},{10,14},{11,15},{16,20},{17,... | collective-permute-start | bytes 27656 | tf_op jit(solution)/shard_map/ppermute | solution.py:22
  48.2 6.5 %collective-permute-start.11 = (f32[3,3,3,1,128]{4,3,0,2,1:T(1,128)}, f32[3,3,3,1,128]{4,3,0,2,1:T(1,128)}, u32[]{:S(2)}, u32[]{:S(2)}) collective-permute-start(f32[3,3,3,1,128]{4,3,0,2,1:T(1,128)} %get-tuple-element.27), channel_id=1, source_target_pairs={{1,0},{2,1},{3,2},{5,4},{6,5},{7,6},{9,8},{10,9},{11,10},{13,12},{... | collective-permute-start | bytes 41480 | tf_op jit(solution)/shard_map/ppermute | solution.py:24
  49.5 5.2 %collective-permute-start.10 = (f32[3,3,3,1,128]{4,3,0,2,1:T(1,128)}, f32[3,3,3,1,128]{4,3,0,2,1:T(1,128)}, u32[]{:S(2)}, u32[]{:S(2)}) collective-permute-start(f32[3,3,3,1,128]{4,3,0,2,1:T(1,128)} %get-tuple-element.28), channel_id=1, source_target_pairs={{0,1},{1,2},{2,3},{4,5},{5,6},{6,7},{8,9},{9,10},{10,11},{12,13},{... | collective-permute-start | bytes 41480 | tf_op jit(solution)/shard_map/ppermute | solution.py:22
  70.1 5.9 %collective-permute-start.13 = (f32[1,1,1,2,128]{4,3,2,1,0:T(2,128)S(1)}, f32[1,1,1,2,128]{4,3,2,1,0:T(2,128)S(1)}, u32[]{:S(2)}, u32[]{:S(2)}) collective-permute-start(f32[1,1,1,2,128]{4,3,2,1,0:T(2,128)S(1)} %bitcast.159), channel_id=1, source_target_pairs={{8,0},{16,8},{24,16},{9,1},{17,9},{25,17},{10,2},{18,10},{26,18},{... | collective-permute-start | bytes 3080 | tf_op jit(solution)/shard_map/ppermute | solution.py:24
  71.4 5.9 %collective-permute-start.12 = (f32[1,1,1,2,128]{4,3,2,1,0:T(2,128)S(1)}, f32[1,1,1,2,128]{4,3,2,1,0:T(2,128)S(1)}, u32[]{:S(2)}, u32[]{:S(2)}) collective-permute-start(f32[1,1,1,2,128]{4,3,2,1,0:T(2,128)S(1)} %bitcast.160), channel_id=1, source_target_pairs={{0,8},{8,16},{16,24},{1,9},{9,17},{17,25},{2,10},{10,18},{18,26},{... | collective-permute-start | bytes 3080 | tf_op jit(solution)/shard_map/ppermute | solution.py:22
  77.3 5.8 %collective-permute-start.15 = (f32[1,3,1,2,128]{4,3,2,1,0:T(2,128)S(1)}, f32[1,3,1,2,128]{4,3,2,1,0:T(2,128)S(1)}, u32[]{:S(2)}, u32[]{:S(2)}) collective-permute-start(f32[1,3,1,2,128]{4,3,2,1,0:T(2,128)S(1)} %pad_maximum_fusion.20), channel_id=1, source_target_pairs={{4,0},{5,1},{6,2},{7,3},{12,8},{13,9},{14,10},{15,11},{20,16},{21,... | collective-permute-start | bytes 9224 | tf_op jit(solution)/shard_map/ppermute | solution.py:24
  78.6 5.9 %collective-permute-start.14 = (f32[1,3,1,2,128]{4,3,2,1,0:T(2,128)S(1)}, f32[1,3,1,2,128]{4,3,2,1,0:T(2,128)S(1)}, u32[]{:S(2)}, u32[]{:S(2)}) collective-permute-start(f32[1,3,1,2,128]{4,3,2,1,0:T(2,128)S(1)} %pad_maximum_fusion.20), channel_id=1, source_target_pairs={{0,4},{1,5},{2,6},{3,7},{8,12},{9,13},{10,14},{11,15},{16,20},{17,... | collective-permute-start | bytes 9224 | tf_op jit(solution)/shard_map/ppermute | solution.py:22
  84.5 2.8 collective-permute-start.16
  86.0 6.6 %collective-permute-start.17 = (f32[1,3,3,1,128]{4,3,2,1,0:T(1,128)S(1)}, f32[1,3,3,1,128]{4,3,2,1,0:T(1,128)S(1)}, u32[]{:S(2)}, u32[]{:S(2)}) collective-permute-start(f32[1,3,3,1,128]{4,3,2,1,0:T(1,128)S(1)} %get-tuple-element.40), channel_id=1, source_target_pairs={{1,0},{2,1},{3,2},{5,4},{6,5},{7,6},{9,8},{10,9},{11,10},{13,12},{... | collective-permute-start | bytes 13832 | tf_op jit(solution)/shard_map/ppermute | solution.py:24
  147.5 5.8 %collective-permute-start.19 = (f32[1,1,1,2,128]{4,3,2,1,0:T(2,128)S(1)}, f32[1,1,1,2,128]{4,3,2,1,0:T(2,128)S(1)}, u32[]{:S(2)}, u32[]{:S(2)}) collective-permute-start(f32[1,1,1,2,128]{4,3,2,1,0:T(2,128)S(1)} %bitcast.148), channel_id=1, source_target_pairs={{8,0},{16,8},{24,16},{9,1},{17,9},{25,17},{10,2},{18,10},{26,18},{... | collective-permute-start | bytes 3080 | tf_op jit(solution)/shard_map/ppermute | solution.py:24
  148.7 5.8 %collective-permute-start.18 = (f32[1,1,1,2,128]{4,3,2,1,0:T(2,128)S(1)}, f32[1,1,1,2,128]{4,3,2,1,0:T(2,128)S(1)}, u32[]{:S(2)}, u32[]{:S(2)}) collective-permute-start(f32[1,1,1,2,128]{4,3,2,1,0:T(2,128)S(1)} %bitcast.149), channel_id=1, source_target_pairs={{0,8},{8,16},{16,24},{1,9},{9,17},{17,25},{2,10},{10,18},{18,26},{... | collective-permute-start | bytes 3080 | tf_op jit(solution)/shard_map/ppermute | solution.py:22
  154.6 5.8 %collective-permute-start.21 = (f32[1,3,1,2,128]{4,3,2,1,0:T(2,128)S(1)}, f32[1,3,1,2,128]{4,3,2,1,0:T(2,128)S(1)}, u32[]{:S(2)}, u32[]{:S(2)}) collective-permute-start(f32[1,3,1,2,128]{4,3,2,1,0:T(2,128)S(1)} %pad_maximum_fusion.21), channel_id=1, source_target_pairs={{4,0},{5,1},{6,2},{7,3},{12,8},{13,9},{14,10},{15,11},{20,16},{21,... | collective-permute-start | bytes 9224 | tf_op jit(solution)/shard_map/ppermute | solution.py:24
  155.9 5.9 %collective-permute-start.20 = (f32[1,3,1,2,128]{4,3,2,1,0:T(2,128)S(1)}, f32[1,3,1,2,128]{4,3,2,1,0:T(2,128)S(1)}, u32[]{:S(2)}, u32[]{:S(2)}) collective-permute-start(f32[1,3,1,2,128]{4,3,2,1,0:T(2,128)S(1)} %pad_maximum_fusion.21), channel_id=1, source_target_pairs={{0,4},{1,5},{2,6},{3,7},{8,12},{9,13},{10,14},{11,15},{16,20},{17,... | collective-permute-start | bytes 9224 | tf_op jit(solution)/shard_map/ppermute | solution.py:22
  161.7 2.6 collective-permute-start.22
  163.0 5.6 %collective-permute-start.23 = (f32[1,3,3,1,128]{4,3,2,1,0:T(1,128)S(1)}, f32[1,3,3,1,128]{4,3,2,1,0:T(1,128)S(1)}, u32[]{:S(2)}, u32[]{:S(2)}) collective-permute-start(f32[1,3,3,1,128]{4,3,2,1,0:T(1,128)S(1)} %get-tuple-element.36), channel_id=1, source_target_pairs={{1,0},{2,1},{3,2},{5,4},{6,5},{7,6},{9,8},{10,9},{11,10},{13,12},{... | collective-permute-start | bytes 13832 | tf_op jit(solution)/shard_map/ppermute | solution.py:24
  227.9 5.8 %collective-permute-start.25 = (f32[1,1,1,2,128]{4,3,2,1,0:T(2,128)S(1)}, f32[1,1,1,2,128]{4,3,2,1,0:T(2,128)S(1)}, u32[]{:S(2)}, u32[]{:S(2)}) collective-permute-start(f32[1,1,1,2,128]{4,3,2,1,0:T(2,128)S(1)} %bitcast.154), channel_id=1, source_target_pairs={{8,0},{16,8},{24,16},{9,1},{17,9},{25,17},{10,2},{18,10},{26,18},{... | collective-permute-start | bytes 3080 | tf_op jit(solution)/shard_map/ppermute | solution.py:24
  229.1 5.8 %collective-permute-start.24 = (f32[1,1,1,2,128]{4,3,2,1,0:T(2,128)S(1)}, f32[1,1,1,2,128]{4,3,2,1,0:T(2,128)S(1)}, u32[]{:S(2)}, u32[]{:S(2)}) collective-permute-start(f32[1,1,1,2,128]{4,3,2,1,0:T(2,128)S(1)} %bitcast.155), channel_id=1, source_target_pairs={{0,8},{8,16},{16,24},{1,9},{9,17},{17,25},{2,10},{10,18},{18,26},{... | collective-permute-start | bytes 3080 | tf_op jit(solution)/shard_map/ppermute | solution.py:22
  235.0 5.8 %collective-permute-start.27 = (f32[1,3,1,2,128]{4,3,2,1,0:T(2,128)S(1)}, f32[1,3,1,2,128]{4,3,2,1,0:T(2,128)S(1)}, u32[]{:S(2)}, u32[]{:S(2)}) collective-permute-start(f32[1,3,1,2,128]{4,3,2,1,0:T(2,128)S(1)} %pad_maximum_fusion.22), channel_id=1, source_target_pairs={{4,0},{5,1},{6,2},{7,3},{12,8},{13,9},{14,10},{15,11},{20,16},{21,... | collective-permute-start | bytes 9224 | tf_op jit(solution)/shard_map/ppermute | solution.py:24
  236.3 5.9 %collective-permute-start.26 = (f32[1,3,1,2,128]{4,3,2,1,0:T(2,128)S(1)}, f32[1,3,1,2,128]{4,3,2,1,0:T(2,128)S(1)}, u32[]{:S(2)}, u32[]{:S(2)}) collective-permute-start(f32[1,3,1,2,128]{4,3,2,1,0:T(2,128)S(1)} %pad_maximum_fusion.22), channel_id=1, source_target_pairs={{0,4},{1,5},{2,6},{3,7},{8,12},{9,13},{10,14},{11,15},{16,20},{17,... | collective-permute-start | bytes 9224 | tf_op jit(solution)/shard_map/ppermute | solution.py:22
  242.7 8.7 %collective-permute-start.28 = (f32[1,3,3,1,128]{4,3,2,1,0:T(1,128)}, f32[1,3,3,1,128]{4,3,2,1,0:T(1,128)}, u32[]{:S(2)}, u32[]{:S(2)}) collective-permute-start(f32[1,3,3,1,128]{4,3,2,1,0:T(1,128)} %get-tuple-element.31), channel_id=1, source_target_pairs={{0,1},{1,2},{2,3},{4,5},{5,6},{6,7},{8,9},{9,10},{10,11},{12,13},{... | collective-permute-start | bytes 13832 | tf_op jit(solution)/shard_map/ppermute | solution.py:22
  244.6 6.8 %collective-permute-start.29 = (f32[1,3,3,1,128]{4,3,2,1,0:T(1,128)}, f32[1,3,3,1,128]{4,3,2,1,0:T(1,128)}, u32[]{:S(2)}, u32[]{:S(2)}) collective-permute-start(f32[1,3,3,1,128]{4,3,2,1,0:T(1,128)} %get-tuple-element.32), channel_id=1, source_target_pairs={{1,0},{2,1},{3,2},{5,4},{6,5},{7,6},{9,8},{10,9},{11,10},{13,12},{... | collective-permute-start | bytes 13832 | tf_op jit(solution)/shard_map/ppermute | solution.py:24
  259.1 59.5 %copy-start.4 = (f32[3,2,128]{2,1,0:T(2,128)S(1)}, f32[3,2,128]{2,1,0:T(2,128)}, u32[]{:S(2)}) copy-start(f32[3,2,128]{2,1,0:T(2,128)} %copy-done.3) | copy-start | bytes 9220
  (35 other events, 506.8 us)
where the time goes:
time: 322 us; the launch traced here: 319 us
  blocking collectives  132 us (41%)
  starting transfers between devices  76 us (24%)
  other arithmetic  41.9 us (13%)
  local copies, waits for them, and re-layouts  32.6 us (10%)
  waiting for transfers between devices  25.9 us (8%)
  between operations  11.2 us (3%)
    psum x3, blocking collectives, paired_sums(): total = lax.psum(pair, ('gx', 'gy', 'gz'))  132 us
    ppermute x15, starting transfers between devices, with_halo(): lax.ppermute(tail, axis, [(i, (i + 1) % count) for i in range(ends)])  56.6 us
    ppermute x15, starting transfers between devices, with_halo(): lax.ppermute(head, axis, [((i + 1) % count, i) for i in range(ends)])  19.5 us
    another operation x15, local copies, waits for them, and re-layouts, neighbours(): return jnp.stack(blocks, axis=1)  19.3 us
    ppermute x15, waiting for transfers between devices, with_halo(): lax.ppermute(head, axis, [((i + 1) % count, i) for i in range(ends)])  13.5 us
    reduce_sum x6, other arithmetic, wsum(): return jnp.sum(weight[None] * near[:, :, None, :], axis=-1)  12.6 us
    ppermute x15, waiting for transfers between devices, with_halo(): lax.ppermute(tail, axis, [(i, (i + 1) % count) for i in range(ends)])  12.3 us
  transfers between devices with their start and end apart: 30, of which 13 were waited for; matrix products, arithmetic and copies ran while one was open for 2% of the time, Pallas kernels for 0%

commit v1 on v0

--- a/solution.py
+++ b/solution.py
@@ -107,7 +107,7 @@
 
     def paired_sums(residual, precond, applied):
         pair = jnp.stack([jnp.sum(residual * precond), jnp.sum(precond * applied)])
-        total = lax.psum(pair, ("gx", "gy", "gz"))
+        total = lax.psum(lax.psum(pair, ("gy", "gz")), "gx")
         return (total[0], total[1])
 
     pressure = jnp.zeros_like(source)

time: 322 us -> 267 us (0.83)
  blocking collectives: 132 us -> 80.6 us
    psum x3 -> x6, blocking collectives: 132 us -> 80.6 us  [paired_sums(): total = lax.psum(lax.psum(pair, ('gy', 'gz')), 'gx')]
  transfers between devices with their start and end apart: 30 -> 30, of which waited for: 13 -> 13; matrix products, arithmetic and copies ran while one was open for 2% -> 3% of each run, Pallas kernels for 0% -> 0%
where the time goes in v1:
time: 267 us; the launch traced here: 264 us
  blocking collectives  80.6 us (30%)
  starting transfers between devices  75.9 us (28%)
  other arithmetic  41.5 us (16%)
  local copies, waits for them, and re-layouts  31.6 us (12%)
  waiting for transfers between devices  23.4 us (9%)
  between operations  11 us (4%)
    psum x6, blocking collectives, paired_sums(): total = lax.psum(lax.psum(pair, ('gy', 'gz')), 'gx')  80.6 us
    ppermute x15, starting transfers between devices, with_halo(): lax.ppermute(tail, axis, [(i, (i + 1) % count) for i in range(ends)])  56.6 us
    ppermute x15, starting transfers between devices, with_halo(): lax.ppermute(head, axis, [((i + 1) % count, i) for i in range(ends)])  19.3 us
    another operation x15, local copies, waits for them, and re-layouts, neighbours(): return jnp.stack(blocks, axis=1)  18.7 us
    reduce_sum x6, other arithmetic, wsum(): return jnp.sum(weight[None] * near[:, :, None, :], axis=-1)  12.5 us
    ppermute x15, waiting for transfers between devices, with_halo(): lax.ppermute(tail, axis, [(i, (i + 1) % count) for i in range(ends)])  12.3 us
    ppermute x15, waiting for transfers between devices, with_halo(): lax.ppermute(head, axis, [((i + 1) % count, i) for i in range(ends)])  11.1 us
  transfers between devices with their start and end apart: 30, of which 13 were waited for; matrix products, arithmetic and copies ran while one was open for 3% of the time, Pallas kernels for 0%

profile of v1, /device:TPU:0, one launch (start us, length us, event | category | flops | bytes accessed | tf_op | source)
XLA Modules:
  0.0 264.0 jit_solution(7161105421806664085)
XLA Ops:
  4.0 5.6 %collective-permute-start = (f32[7,1,1,2,128]{4,0,3,2,1:T(8,128)S(1)}, f32[7,1,1,2,128]{4,0,3,2,1:T(8,128)S(1)}, u32[]{:S(2)}, u32[]{:S(2)}) collective-permute-start(f32[7,1,1,2,128]{4,0,3,2,1:T(8,128)S(1)} %pad_maximum_fusion.19), channel_id=1, source_target_pairs={{0,8},{8,16},{16,24},{1,9},{9,17},{17,25},{2,10},{10,18},{18,26},{... | collective-permute-start | bytes 21512 | tf_op jit(solution)/shard_map/ppermute | solution.py:22
  12.3 4.5 %collective-permute-start.2 = (f32[7,3,1,2,128]{4,0,3,2,1:T(8,128)S(1)}, f32[7,3,1,2,128]{4,0,3,2,1:T(8,128)S(1)}, u32[]{:S(2)}, u32[]{:S(2)}) collective-permute-start(f32[7,3,1,2,128]{4,0,3,2,1:T(8,128)S(1)} %pad_maximum_fusion.11), channel_id=1, source_target_pairs={{0,4},{1,5},{2,6},{3,7},{8,12},{9,13},{10,14},{11,15},{16,20},{17,... | collective-permute-start | bytes 64520 | tf_op jit(solution)/shard_map/ppermute | solution.py:22
  21.0 3.9 %collective-permute-done.5 = f32[7,3,3,1,128]{4,0,3,2,1:T(8,128)S(1)} collective-permute-done((f32[7,3,3,1,128]{4,0,3,2,1:T(8,128)S(1)}, f32[7,3,3,1,128]{4,0,3,2,1:T(8,128)S(1)}, u32[]{:S(2)}, u32[]{:S(2)}) %collective-permute-start.5) | collective-permute-done | bytes 32288 | tf_op jit(solution)/shard_map/ppermute | solution.py:24
  25.3 1.5 broadcast_subtract_fusion
  26.9 1.6 fusion.6
  28.9 1.7 copy-done
  30.6 1.8 multiply_reduce_fusion
  33.9 4.8 %collective-permute-start.6 = (f32[3,1,1,2,128]{4,3,0,2,1:T(2,128)S(1)}, f32[3,1,1,2,128]{4,3,0,2,1:T(2,128)S(1)}, u32[]{:S(2)}, u32[]{:S(2)}) collective-permute-start(f32[3,1,1,2,128]{4,3,0,2,1:T(2,128)S(1)} %bitcast.144), channel_id=1, source_target_pairs={{0,8},{8,16},{16,24},{1,9},{9,17},{17,25},{2,10},{10,18},{18,26},{... | collective-permute-start | bytes 9224 | tf_op jit(solution)/shard_map/ppermute | solution.py:22
  41.3 4.5 %collective-permute-start.8 = (f32[3,3,1,2,128]{4,3,0,2,1:T(2,128)S(1)}, f32[3,3,1,2,128]{4,3,0,2,1:T(2,128)S(1)}, u32[]{:S(2)}, u32[]{:S(2)}) collective-permute-start(f32[3,3,1,2,128]{4,3,0,2,1:T(2,128)S(1)} %pad_maximum_fusion.15), channel_id=1, source_target_pairs={{0,4},{1,5},{2,6},{3,7},{8,12},{9,13},{10,14},{11,15},{16,20},{17,... | collective-permute-start | bytes 27656 | tf_op jit(solution)/shard_map/ppermute | solution.py:22
  49.2 3.8 %collective-permute-start.10 = (f32[3,3,3,1,128]{4,3,0,2,1:T(1,128)}, f32[3,3,3,1,128]{4,3,0,2,1:T(1,128)}, u32[]{:S(2)}, u32[]{:S(2)}) collective-permute-start(f32[3,3,3,1,128]{4,3,0,2,1:T(1,128)} %get-tuple-element.28), channel_id=1, source_target_pairs={{0,1},{1,2},{2,3},{4,5},{5,6},{6,7},{8,9},{9,10},{10,11},{12,13},{... | collective-permute-start | bytes 41480 | tf_op jit(solution)/shard_map/ppermute | solution.py:22
  54.3 1.5 pad_maximum_fusion.5
  56.4 1.5 stack_reshape.32
  65.8 3.3 %multiply_reduce_fusion.2 = f32[4,2,128]{2,1,0:T(2,128)S(1)} fusion(f32[4,2,3456]{2,1,0:T(2,128)S(1)} %copy.34, f32[2,128,3456]{2,1,0:T(8,128)} %copy-done), kind=kLoop, calls=%fused_computation.2 | loop fusion | flops 7076864 | bytes 3653632 | tf_op jit(solution)/shard_map/reduce_sum | solution.py:47
  71.0 4.6 %collective-permute-start.12 = (f32[1,1,1,2,128]{4,3,2,1,0:T(2,128)S(1)}, f32[1,1,1,2,128]{4,3,2,1,0:T(2,128)S(1)}, u32[]{:S(2)}, u32[]{:S(2)}) collective-permute-start(f32[1,1,1,2,128]{4,3,2,1,0:T(2,128)S(1)} %bitcast.160), channel_id=1, source_target_pairs={{0,8},{8,16},{16,24},{1,9},{9,17},{17,25},{2,10},{10,18},{18,26},{... | collective-permute-start | bytes 3080 | tf_op jit(solution)/shard_map/ppermute | solution.py:22
  78.3 4.5 %collective-permute-start.14 = (f32[1,3,1,2,128]{4,3,2,1,0:T(2,128)S(1)}, f32[1,3,1,2,128]{4,3,2,1,0:T(2,128)S(1)}, u32[]{:S(2)}, u32[]{:S(2)}) collective-permute-start(f32[1,3,1,2,128]{4,3,2,1,0:T(2,128)S(1)} %pad_maximum_fusion.20), channel_id=1, source_target_pairs={{0,4},{1,5},{2,6},{3,7},{8,12},{9,13},{10,14},{11,15},{16,20},{17,... | collective-permute-start | bytes 9224 | tf_op jit(solution)/shard_map/ppermute | solution.py:22
  84.1 1.5 collective-permute-start.16
  86.9 5.3 %collective-permute-done.17 = f32[1,3,3,1,128]{4,3,2,1,0:T(1,128)S(1)} collective-permute-done((f32[1,3,3,1,128]{4,3,2,1,0:T(1,128)S(1)}, f32[1,3,3,1,128]{4,3,2,1,0:T(1,128)S(1)}, u32[]{:S(2)}, u32[]{:S(2)}) %collective-permute-start.17) | collective-permute-done | bytes 4640 | tf_op jit(solution)/shard_map/ppermute | solution.py:24
  98.4 1.8 pad_maximum_fusion.23
  100.2 15.0 %psum.42 = f32[2]{0:T(128)} all-reduce(f32[2]{0:T(128)} %pad_maximum_fusion.23), channel_id=1, replica_groups=mesh['gx'=4,'gy'=2,'gz'=4] {'gy','gz'}, use_global_device_ids=true, to_apply=%region_9.0 | all-reduce | flops 2 | bytes 16 | tf_op jit(solution)/shard_map/psum | solution.py:110
  115.3 14.2 %psum.43 = f32[2]{0:T(128)} all-reduce(f32[2]{0:T(128)} %psum.42), channel_id=1, replica_groups=mesh['gx'=4,'gy'=2,'gz'=4] {'gx'}, use_global_device_ids=true, to_apply=%region_10.0 | all-reduce | flops 2 | bytes 16 | tf_op jit(solution)/shard_map/psum | solution.py:110
  134.1 4.5 %collective-permute-start.18 = (f32[1,1,1,2,128]{4,3,2,1,0:T(2,128)S(1)}, f32[1,1,1,2,128]{4,3,2,1,0:T(2,128)S(1)}, u32[]{:S(2)}, u32[]{:S(2)}) collective-permute-start(f32[1,1,1,2,128]{4,3,2,1,0:T(2,128)S(1)} %bitcast.149), channel_id=1, source_target_pairs={{0,8},{8,16},{16,24},{1,9},{9,17},{17,25},{2,10},{10,18},{18,26},{... | collective-permute-start | bytes 3080 | tf_op jit(solution)/shard_map/ppermute | solution.py:22
  141.2 4.5 %collective-permute-start.20 = (f32[1,3,1,2,128]{4,3,2,1,0:T(2,128)S(1)}, f32[1,3,1,2,128]{4,3,2,1,0:T(2,128)S(1)}, u32[]{:S(2)}, u32[]{:S(2)}) collective-permute-start(f32[1,3,1,2,128]{4,3,2,1,0:T(2,128)S(1)} %pad_maximum_fusion.21), channel_id=1, source_target_pairs={{0,4},{1,5},{2,6},{3,7},{8,12},{9,13},{10,14},{11,15},{16,20},{17,... | collective-permute-start | bytes 9224 | tf_op jit(solution)/shard_map/ppermute | solution.py:22
  149.7 1.8 collective-permute-done.23
  158.3 1.7 pad_maximum_fusion.24
  160.1 14.9 %psum.44 = f32[2]{0:T(128)} all-reduce(f32[2]{0:T(128)} %pad_maximum_fusion.24), channel_id=1, replica_groups=mesh['gx'=4,'gy'=2,'gz'=4] {'gy','gz'}, use_global_device_ids=true, to_apply=%region_14.0 | all-reduce | flops 2 | bytes 16 | tf_op jit(solution)/shard_map/psum | solution.py:110
  175.0 11.2 %psum.45 = f32[2]{0:T(128)} all-reduce(f32[2]{0:T(128)} %psum.44), channel_id=1, replica_groups=mesh['gx'=4,'gy'=2,'gz'=4] {'gx'}, use_global_device_ids=true, to_apply=%region_15.0 | all-reduce | flops 2 | bytes 16 | tf_op jit(solution)/shard_map/psum | solution.py:110
  194.4 4.5 %collective-permute-start.24 = (f32[1,1,1,2,128]{4,3,2,1,0:T(2,128)S(1)}, f32[1,1,1,2,128]{4,3,2,1,0:T(2,128)S(1)}, u32[]{:S(2)}, u32[]{:S(2)}) collective-permute-start(f32[1,1,1,2,128]{4,3,2,1,0:T(2,128)S(1)} %bitcast.155), channel_id=1, source_target_pairs={{0,8},{8,16},{16,24},{1,9},{9,17},{17,25},{2,10},{10,18},{18,26},{... | collective-permute-start | bytes 3080 | tf_op jit(solution)/shard_map/ppermute | solution.py:22
  201.6 4.5 %collective-permute-start.26 = (f32[1,3,1,2,128]{4,3,2,1,0:T(2,128)S(1)}, f32[1,3,1,2,128]{4,3,2,1,0:T(2,128)S(1)}, u32[]{:S(2)}, u32[]{:S(2)}) collective-permute-start(f32[1,3,1,2,128]{4,3,2,1,0:T(2,128)S(1)} %pad_maximum_fusion.22), channel_id=1, source_target_pairs={{0,4},{1,5},{2,6},{3,7},{8,12},{9,13},{10,14},{11,15},{16,20},{17,... | collective-permute-start | bytes 9224 | tf_op jit(solution)/shard_map/ppermute | solution.py:22
  208.0 1.9 collective-permute-start.28
  226.3 14.7 %psum.46 = f32[2]{0:T(128)S(1)} all-reduce(f32[2]{0:T(128)S(1)} %pad_maximum_fusion.25), channel_id=1, replica_groups=mesh['gx'=4,'gy'=2,'gz'=4] {'gy','gz'}, use_global_device_ids=true, to_apply=%region_19.0 | all-reduce | flops 2 | bytes 16 | tf_op jit(solution)/shard_map/psum | solution.py:110
  241.7 10.6 %psum.47 = f32[2]{0:T(128)S(1)} all-reduce(f32[2]{0:T(128)S(1)} %psum.46), channel_id=1, replica_groups=mesh['gx'=4,'gy'=2,'gz'=4] {'gx'}, use_global_device_ids=true, to_apply=%region_20.0 | all-reduce | flops 2 | bytes 16 | tf_op jit(solution)/shard_map/psum | solution.py:110
  260.2 3.1 %multiply_reduce_fusion.1 = f32[4,2,128]{2,1,0:T(2,128)S(1)} fusion(f32[4,2,3456]{2,1,0:T(2,128)S(1)} %copy.41, f32[2,128,3456]{2,1,0:T(8,128)} %copy-done), kind=kLoop, calls=%fused_computation.1 | loop fusion | flops 7076864 | bytes 3653632 | tf_op jit(solution)/shard_map/reduce_sum | solution.py:47
  (201 shorter events, 87.8 us)
Async XLA Ops:
  2.7 7.6 %collective-permute-start.1 = (f32[7,1,1,2,128]{4,0,3,2,1:T(8,128)S(1)}, f32[7,1,1,2,128]{4,0,3,2,1:T(8,128)S(1)}, u32[]{:S(2)}, u32[]{:S(2)}) collective-permute-start(f32[7,1,1,2,128]{4,0,3,2,1:T(8,128)S(1)} %pad_maximum_fusion.19), channel_id=1, source_target_pairs={{8,0},{16,8},{24,16},{9,1},{17,9},{25,17},{10,2},{18,10},{26,18},{... | collective-permute-start | bytes 21512 | tf_op jit(solution)/shard_map/ppermute | solution.py:24
  4.0 6.9 %collective-permute-start = (f32[7,1,1,2,128]{4,0,3,2,1:T(8,128)S(1)}, f32[7,1,1,2,128]{4,0,3,2,1:T(8,128)S(1)}, u32[]{:S(2)}, u32[]{:S(2)}) collective-permute-start(f32[7,1,1,2,128]{4,0,3,2,1:T(8,128)S(1)} %pad_maximum_fusion.19), channel_id=1, source_target_pairs={{0,8},{8,16},{16,24},{1,9},{9,17},{17,25},{2,10},{10,18},{18,26},{... | collective-permute-start | bytes 21512 | tf_op jit(solution)/shard_map/ppermute | solution.py:22
  11.0 5.9 %collective-permute-start.3 = (f32[7,3,1,2,128]{4,0,3,2,1:T(8,128)S(1)}, f32[7,3,1,2,128]{4,0,3,2,1:T(8,128)S(1)}, u32[]{:S(2)}, u32[]{:S(2)}) collective-permute-start(f32[7,3,1,2,128]{4,0,3,2,1:T(8,128)S(1)} %pad_maximum_fusion.11), channel_id=1, source_target_pairs={{4,0},{5,1},{6,2},{7,3},{12,8},{13,9},{14,10},{15,11},{20,16},{21,... | collective-permute-start | bytes 64520 | tf_op jit(solution)/shard_map/ppermute | solution.py:24
  12.3 6.1 %collective-permute-start.2 = (f32[7,3,1,2,128]{4,0,3,2,1:T(8,128)S(1)}, f32[7,3,1,2,128]{4,0,3,2,1:T(8,128)S(1)}, u32[]{:S(2)}, u32[]{:S(2)}) collective-permute-start(f32[7,3,1,2,128]{4,0,3,2,1:T(8,128)S(1)} %pad_maximum_fusion.11), channel_id=1, source_target_pairs={{0,4},{1,5},{2,6},{3,7},{8,12},{9,13},{10,14},{11,15},{16,20},{17,... | collective-permute-start | bytes 64520 | tf_op jit(solution)/shard_map/ppermute | solution.py:22
  18.3 2.6 collective-permute-start.4
  19.6 5.3 %collective-permute-start.5 = (f32[7,3,3,1,128]{4,0,3,2,1:T(8,128)S(1)}, f32[7,3,3,1,128]{4,0,3,2,1:T(8,128)S(1)}, u32[]{:S(2)}, u32[]{:S(2)}) collective-permute-start(f32[7,3,3,1,128]{4,0,3,2,1:T(8,128)S(1)} %get-tuple-element.24), channel_id=1, source_target_pairs={{1,0},{2,1},{3,2},{5,4},{6,5},{7,6},{9,8},{10,9},{11,10},{13,12},{... | collective-permute-start | bytes 96776 | tf_op jit(solution)/shard_map/ppermute | solution.py:24
  28.5 40.7 %copy-start.5 = (f32[2,128]{1,0:T(2,128)}, f32[2,128]{1,0:T(2,128)S(1)}, u32[]{:S(2)}) copy-start(f32[2,128]{1,0:T(2,128)S(1)} %get-tuple-element.17) | copy-start | bytes 3076
  32.6 60.3 %copy-start.3 = (f32[3,2,128]{2,1,0:T(2,128)}, f32[3,2,128]{2,1,0:T(2,128)S(1)}, u32[]{:S(2)}) copy-start(f32[3,2,128]{2,1,0:T(2,128)S(1)} %fusion.20) | copy-start | bytes 9220
  32.6 6.1 %collective-permute-start.7 = (f32[3,1,1,2,128]{4,3,0,2,1:T(2,128)S(1)}, f32[3,1,1,2,128]{4,3,0,2,1:T(2,128)S(1)}, u32[]{:S(2)}, u32[]{:S(2)}) collective-permute-start(f32[3,1,1,2,128]{4,3,0,2,1:T(2,128)S(1)} %bitcast.143), channel_id=1, source_target_pairs={{8,0},{16,8},{24,16},{9,1},{17,9},{25,17},{10,2},{18,10},{26,18},{... | collective-permute-start | bytes 9224 | tf_op jit(solution)/shard_map/ppermute | solution.py:24
  33.9 6.1 %collective-permute-start.6 = (f32[3,1,1,2,128]{4,3,0,2,1:T(2,128)S(1)}, f32[3,1,1,2,128]{4,3,0,2,1:T(2,128)S(1)}, u32[]{:S(2)}, u32[]{:S(2)}) collective-permute-start(f32[3,1,1,2,128]{4,3,0,2,1:T(2,128)S(1)} %bitcast.144), channel_id=1, source_target_pairs={{0,8},{8,16},{16,24},{1,9},{9,17},{17,25},{2,10},{10,18},{18,26},{... | collective-permute-start | bytes 9224 | tf_op jit(solution)/shard_map/ppermute | solution.py:22
  40.0 5.9 %collective-permute-start.9 = (f32[3,3,1,2,128]{4,3,0,2,1:T(2,128)S(1)}, f32[3,3,1,2,128]{4,3,0,2,1:T(2,128)S(1)}, u32[]{:S(2)}, u32[]{:S(2)}) collective-permute-start(f32[3,3,1,2,128]{4,3,0,2,1:T(2,128)S(1)} %pad_maximum_fusion.15), channel_id=1, source_target_pairs={{4,0},{5,1},{6,2},{7,3},{12,8},{13,9},{14,10},{15,11},{20,16},{21,... | collective-permute-start | bytes 27656 | tf_op jit(solution)/shard_map/ppermute | solution.py:24
  41.3 5.9 %collective-permute-start.8 = (f32[3,3,1,2,128]{4,3,0,2,1:T(2,128)S(1)}, f32[3,3,1,2,128]{4,3,0,2,1:T(2,128)S(1)}, u32[]{:S(2)}, u32[]{:S(2)}) collective-permute-start(f32[3,3,1,2,128]{4,3,0,2,1:T(2,128)S(1)} %pad_maximum_fusion.15), channel_id=1, source_target_pairs={{0,4},{1,5},{2,6},{3,7},{8,12},{9,13},{10,14},{11,15},{16,20},{17,... | collective-permute-start | bytes 27656 | tf_op jit(solution)/shard_map/ppermute | solution.py:22
  47.9 6.5 %collective-permute-start.11 = (f32[3,3,3,1,128]{4,3,0,2,1:T(1,128)}, f32[3,3,3,1,128]{4,3,0,2,1:T(1,128)}, u32[]{:S(2)}, u32[]{:S(2)}) collective-permute-start(f32[3,3,3,1,128]{4,3,0,2,1:T(1,128)} %get-tuple-element.27), channel_id=1, source_target_pairs={{1,0},{2,1},{3,2},{5,4},{6,5},{7,6},{9,8},{10,9},{11,10},{13,12},{... | collective-permute-start | bytes 41480 | tf_op jit(solution)/shard_map/ppermute | solution.py:24
  49.2 5.2 %collective-permute-start.10 = (f32[3,3,3,1,128]{4,3,0,2,1:T(1,128)}, f32[3,3,3,1,128]{4,3,0,2,1:T(1,128)}, u32[]{:S(2)}, u32[]{:S(2)}) collective-permute-start(f32[3,3,3,1,128]{4,3,0,2,1:T(1,128)} %get-tuple-element.28), channel_id=1, source_target_pairs={{0,1},{1,2},{2,3},{4,5},{5,6},{6,7},{8,9},{9,10},{10,11},{12,13},{... | collective-permute-start | bytes 41480 | tf_op jit(solution)/shard_map/ppermute | solution.py:22
  69.8 5.9 %collective-permute-start.13 = (f32[1,1,1,2,128]{4,3,2,1,0:T(2,128)S(1)}, f32[1,1,1,2,128]{4,3,2,1,0:T(2,128)S(1)}, u32[]{:S(2)}, u32[]{:S(2)}) collective-permute-start(f32[1,1,1,2,128]{4,3,2,1,0:T(2,128)S(1)} %bitcast.159), channel_id=1, source_target_pairs={{8,0},{16,8},{24,16},{9,1},{17,9},{25,17},{10,2},{18,10},{26,18},{... | collective-permute-start | bytes 3080 | tf_op jit(solution)/shard_map/ppermute | solution.py:24
  71.0 5.9 %collective-permute-start.12 = (f32[1,1,1,2,128]{4,3,2,1,0:T(2,128)S(1)}, f32[1,1,1,2,128]{4,3,2,1,0:T(2,128)S(1)}, u32[]{:S(2)}, u32[]{:S(2)}) collective-permute-start(f32[1,1,1,2,128]{4,3,2,1,0:T(2,128)S(1)} %bitcast.160), channel_id=1, source_target_pairs={{0,8},{8,16},{16,24},{1,9},{9,17},{17,25},{2,10},{10,18},{18,26},{... | collective-permute-start | bytes 3080 | tf_op jit(solution)/shard_map/ppermute | solution.py:22
  77.0 5.8 %collective-permute-start.15 = (f32[1,3,1,2,128]{4,3,2,1,0:T(2,128)S(1)}, f32[1,3,1,2,128]{4,3,2,1,0:T(2,128)S(1)}, u32[]{:S(2)}, u32[]{:S(2)}) collective-permute-start(f32[1,3,1,2,128]{4,3,2,1,0:T(2,128)S(1)} %pad_maximum_fusion.20), channel_id=1, source_target_pairs={{4,0},{5,1},{6,2},{7,3},{12,8},{13,9},{14,10},{15,11},{20,16},{21,... | collective-permute-start | bytes 9224 | tf_op jit(solution)/shard_map/ppermute | solution.py:24
  78.3 5.9 %collective-permute-start.14 = (f32[1,3,1,2,128]{4,3,2,1,0:T(2,128)S(1)}, f32[1,3,1,2,128]{4,3,2,1,0:T(2,128)S(1)}, u32[]{:S(2)}, u32[]{:S(2)}) collective-permute-start(f32[1,3,1,2,128]{4,3,2,1,0:T(2,128)S(1)} %pad_maximum_fusion.20), channel_id=1, source_target_pairs={{0,4},{1,5},{2,6},{3,7},{8,12},{9,13},{10,14},{11,15},{16,20},{17,... | collective-permute-start | bytes 9224 | tf_op jit(solution)/shard_map/ppermute | solution.py:22
  84.1 2.8 %collective-permute-start.16 = (f32[1,3,3,1,128]{4,3,2,1,0:T(1,128)S(1)}, f32[1,3,3,1,128]{4,3,2,1,0:T(1,128)S(1)}, u32[]{:S(2)}, u32[]{:S(2)}) collective-permute-start(f32[1,3,3,1,128]{4,3,2,1,0:T(1,128)S(1)} %get-tuple-element.39), channel_id=1, source_target_pairs={{0,1},{1,2},{2,3},{4,5},{5,6},{6,7},{8,9},{9,10},{10,11},{12,13},{... | collective-permute-start | bytes 13832 | tf_op jit(solution)/shard_map/ppermute | solution.py:22
  85.6 6.6 %collective-permute-start.17 = (f32[1,3,3,1,128]{4,3,2,1,0:T(1,128)S(1)}, f32[1,3,3,1,128]{4,3,2,1,0:T(1,128)S(1)}, u32[]{:S(2)}, u32[]{:S(2)}) collective-permute-start(f32[1,3,3,1,128]{4,3,2,1,0:T(1,128)S(1)} %get-tuple-element.40), channel_id=1, source_target_pairs={{1,0},{2,1},{3,2},{5,4},{6,5},{7,6},{9,8},{10,9},{11,10},{13,12},{... | collective-permute-start | bytes 13832 | tf_op jit(solution)/shard_map/ppermute | solution.py:24
  132.8 5.8 %collective-permute-start.19 = (f32[1,1,1,2,128]{4,3,2,1,0:T(2,128)S(1)}, f32[1,1,1,2,128]{4,3,2,1,0:T(2,128)S(1)}, u32[]{:S(2)}, u32[]{:S(2)}) collective-permute-start(f32[1,1,1,2,128]{4,3,2,1,0:T(2,128)S(1)} %bitcast.148), channel_id=1, source_target_pairs={{8,0},{16,8},{24,16},{9,1},{17,9},{25,17},{10,2},{18,10},{26,18},{... | collective-permute-start | bytes 3080 | tf_op jit(solution)/shard_map/ppermute | solution.py:24
  134.1 5.8 %collective-permute-start.18 = (f32[1,1,1,2,128]{4,3,2,1,0:T(2,128)S(1)}, f32[1,1,1,2,128]{4,3,2,1,0:T(2,128)S(1)}, u32[]{:S(2)}, u32[]{:S(2)}) collective-permute-start(f32[1,1,1,2,128]{4,3,2,1,0:T(2,128)S(1)} %bitcast.149), channel_id=1, source_target_pairs={{0,8},{8,16},{16,24},{1,9},{9,17},{17,25},{2,10},{10,18},{18,26},{... | collective-permute-start | bytes 3080 | tf_op jit(solution)/shard_map/ppermute | solution.py:22
  139.9 5.8 %collective-permute-start.21 = (f32[1,3,1,2,128]{4,3,2,1,0:T(2,128)S(1)}, f32[1,3,1,2,128]{4,3,2,1,0:T(2,128)S(1)}, u32[]{:S(2)}, u32[]{:S(2)}) collective-permute-start(f32[1,3,1,2,128]{4,3,2,1,0:T(2,128)S(1)} %pad_maximum_fusion.21), channel_id=1, source_target_pairs={{4,0},{5,1},{6,2},{7,3},{12,8},{13,9},{14,10},{15,11},{20,16},{21,... | collective-permute-start | bytes 9224 | tf_op jit(solution)/shard_map/ppermute | solution.py:24
  141.2 5.9 %collective-permute-start.20 = (f32[1,3,1,2,128]{4,3,2,1,0:T(2,128)S(1)}, f32[1,3,1,2,128]{4,3,2,1,0:T(2,128)S(1)}, u32[]{:S(2)}, u32[]{:S(2)}) collective-permute-start(f32[1,3,1,2,128]{4,3,2,1,0:T(2,128)S(1)} %pad_maximum_fusion.21), channel_id=1, source_target_pairs={{0,4},{1,5},{2,6},{3,7},{8,12},{9,13},{10,14},{11,15},{16,20},{17,... | collective-permute-start | bytes 9224 | tf_op jit(solution)/shard_map/ppermute | solution.py:22
  147.1 2.6 collective-permute-start.22
  148.4 3.1 %collective-permute-start.23 = (f32[1,3,3,1,128]{4,3,2,1,0:T(1,128)S(1)}, f32[1,3,3,1,128]{4,3,2,1,0:T(1,128)S(1)}, u32[]{:S(2)}, u32[]{:S(2)}) collective-permute-start(f32[1,3,3,1,128]{4,3,2,1,0:T(1,128)S(1)} %get-tuple-element.36), channel_id=1, source_target_pairs={{1,0},{2,1},{3,2},{5,4},{6,5},{7,6},{9,8},{10,9},{11,10},{13,12},{... | collective-permute-start | bytes 13832 | tf_op jit(solution)/shard_map/ppermute | solution.py:24
  193.1 5.8 %collective-permute-start.25 = (f32[1,1,1,2,128]{4,3,2,1,0:T(2,128)S(1)}, f32[1,1,1,2,128]{4,3,2,1,0:T(2,128)S(1)}, u32[]{:S(2)}, u32[]{:S(2)}) collective-permute-start(f32[1,1,1,2,128]{4,3,2,1,0:T(2,128)S(1)} %bitcast.154), channel_id=1, source_target_pairs={{8,0},{16,8},{24,16},{9,1},{17,9},{25,17},{10,2},{18,10},{26,18},{... | collective-permute-start | bytes 3080 | tf_op jit(solution)/shard_map/ppermute | solution.py:24
  194.4 5.8 %collective-permute-start.24 = (f32[1,1,1,2,128]{4,3,2,1,0:T(2,128)S(1)}, f32[1,1,1,2,128]{4,3,2,1,0:T(2,128)S(1)}, u32[]{:S(2)}, u32[]{:S(2)}) collective-permute-start(f32[1,1,1,2,128]{4,3,2,1,0:T(2,128)S(1)} %bitcast.155), channel_id=1, source_target_pairs={{0,8},{8,16},{16,24},{1,9},{9,17},{17,25},{2,10},{10,18},{18,26},{... | collective-permute-start | bytes 3080 | tf_op jit(solution)/shard_map/ppermute | solution.py:22
  200.3 5.8 %collective-permute-start.27 = (f32[1,3,1,2,128]{4,3,2,1,0:T(2,128)S(1)}, f32[1,3,1,2,128]{4,3,2,1,0:T(2,128)S(1)}, u32[]{:S(2)}, u32[]{:S(2)}) collective-permute-start(f32[1,3,1,2,128]{4,3,2,1,0:T(2,128)S(1)} %pad_maximum_fusion.22), channel_id=1, source_target_pairs={{4,0},{5,1},{6,2},{7,3},{12,8},{13,9},{14,10},{15,11},{20,16},{21,... | collective-permute-start | bytes 9224 | tf_op jit(solution)/shard_map/ppermute | solution.py:24
  201.6 5.9 %collective-permute-start.26 = (f32[1,3,1,2,128]{4,3,2,1,0:T(2,128)S(1)}, f32[1,3,1,2,128]{4,3,2,1,0:T(2,128)S(1)}, u32[]{:S(2)}, u32[]{:S(2)}) collective-permute-start(f32[1,3,1,2,128]{4,3,2,1,0:T(2,128)S(1)} %pad_maximum_fusion.22), channel_id=1, source_target_pairs={{0,4},{1,5},{2,6},{3,7},{8,12},{9,13},{10,14},{11,15},{16,20},{17,... | collective-permute-start | bytes 9224 | tf_op jit(solution)/shard_map/ppermute | solution.py:22
  208.0 8.5 %collective-permute-start.28 = (f32[1,3,3,1,128]{4,3,2,1,0:T(1,128)}, f32[1,3,3,1,128]{4,3,2,1,0:T(1,128)}, u32[]{:S(2)}, u32[]{:S(2)}) collective-permute-start(f32[1,3,3,1,128]{4,3,2,1,0:T(1,128)} %get-tuple-element.31), channel_id=1, source_target_pairs={{0,1},{1,2},{2,3},{4,5},{5,6},{6,7},{8,9},{9,10},{10,11},{12,13},{... | collective-permute-start | bytes 13832 | tf_op jit(solution)/shard_map/ppermute | solution.py:22
  209.9 6.7 %collective-permute-start.29 = (f32[1,3,3,1,128]{4,3,2,1,0:T(1,128)}, f32[1,3,3,1,128]{4,3,2,1,0:T(1,128)}, u32[]{:S(2)}, u32[]{:S(2)}) collective-permute-start(f32[1,3,3,1,128]{4,3,2,1,0:T(1,128)} %get-tuple-element.32), channel_id=1, source_target_pairs={{1,0},{2,1},{3,2},{5,4},{6,5},{7,6},{9,8},{10,9},{11,10},{13,12},{... | collective-permute-start | bytes 13832 | tf_op jit(solution)/shard_map/ppermute | solution.py:24
  (35 other events, 427.5 us)
